TPU v7x, 32 devices: a whole 2x2x4 slice. The times are simulated.
32 devices in a mesh: ctx: 4 (over x, core), ep: 8 (over z, y).
Axes of the slice: x: 2, y: 2, z: 4, core: 2. Of those that a mesh axis runs over, the one named last changes fastest.
Arguments:
- query_latent: bfloat16 [1, 512, 128, 512], P(None, 'ctx', 'ep'), may hold values from -6 to 6
- query_rope: bfloat16 [1, 128, 64, 512], P(None, 'ep', None, 'ctx'), may hold values from -12 to 12
- key_latent: bfloat16 [1, 512, 512], P(None, 'ctx'), may hold values from -6 to 6
- key_rope: bfloat16 [1, 64, 512], P(None, None, 'ctx'), may hold values from -14 to 14
- output_grad: bfloat16 [1, 512, 128, 512], P(None, 'ctx', 'ep'), may hold values from -6 to 6
Outputs:
- attended: bfloat16 [1, 512, 128, 512], P(None, 'ctx', 'ep')
- query_latent_grad: bfloat16 [1, 512, 128, 512], P(None, 'ctx', 'ep')
- query_rope_grad: bfloat16 [1, 128, 64, 512], P(None, 'ep', None, 'ctx')
- key_latent_grad: bfloat16 [1, 512, 512], P(None, 'ctx')
- key_rope_grad: bfloat16 [1, 64, 512], P(None, None, 'ctx')
All inputs are finite; a program needn't handle non-finite values.
Results may differ from a plain program's by a relative error of at most 0.018.
Values may be sent and summed in bfloat16 or wider, within the bound.
No kernel may reach another device: no remote copies, remote signals or barrier semaphores. Data moves between devices by JAX's collectives and lax.ppermute only.
A program may use at most 64 MiB of HBM per device.

v0:
```python
import jax
import jax.numpy as jnp
from jax import lax
from jax.sharding import PartitionSpec as P

scale_factor = 192.0 ** (-0.5)


def body(query_latent, query_rope, key_latent, key_rope, output_grad):
    block_len = query_latent.shape[1]
    whole_latent, whole_rope = (
        lax.all_gather(key_latent, "ctx", axis=1, tiled=True),
        lax.all_gather(key_rope, "ctx", axis=2, tiled=True),
    )
    length = whole_latent.shape[1]
    offset = lax.axis_index("ctx") * block_len
    query_place = offset + jnp.arange(block_len, dtype=jnp.int32)
    allowed = jnp.arange(length, dtype=jnp.int32)[None, :] <= query_place[:, None]
    scores = jnp.einsum(
        "sthd,sjd->shtj", query_latent, whole_latent, preferred_element_type=jnp.float32
    )
    scores = scores + jnp.einsum(
        "shdt,sdj->shtj", query_rope, whole_rope, preferred_element_type=jnp.float32
    )
    scores = jnp.where(allowed, scores * scale_factor, jnp.float32(-1e30))
    row_max = jnp.max(scores, axis=-1, keepdims=True)
    powers = jnp.exp(scores - row_max)
    weights = powers / jnp.sum(powers, axis=-1, keepdims=True)
    rounded_weights = weights.astype(jnp.bfloat16)
    attended = jnp.einsum(
        "shtj,sjd->sthd", rounded_weights, whole_latent, preferred_element_type=jnp.float32
    ).astype(jnp.bfloat16)
    row_dots = jnp.einsum(
        "sthd,sthd->sht", output_grad, attended, preferred_element_type=jnp.float32
    )
    weight_grad = jnp.einsum(
        "sthd,sjd->shtj", output_grad, whole_latent, preferred_element_type=jnp.float32
    )
    score_grad = (weights * (weight_grad - row_dots[..., None])).astype(jnp.bfloat16)
    latent_qgrad = (
        scale_factor
        * jnp.einsum("shtj,sjd->sthd", score_grad, whole_latent, preferred_element_type=jnp.float32)
    ).astype(jnp.bfloat16)
    rope_qgrad = (
        scale_factor
        * jnp.einsum("shtj,sdj->shdt", score_grad, whole_rope, preferred_element_type=jnp.float32)
    ).astype(jnp.bfloat16)
    latent_term = scale_factor * jnp.einsum(
        "shtj,sthd->sjd", score_grad, query_latent, preferred_element_type=jnp.float32
    )
    latent_term = latent_term + jnp.einsum(
        "shtj,sthd->sjd", rounded_weights, output_grad, preferred_element_type=jnp.float32
    )
    rope_term = scale_factor * jnp.einsum(
        "shtj,shdt->sdj", score_grad, query_rope, preferred_element_type=jnp.float32
    )
    latent_part, rope_part = (
        lax.psum_scatter(
            latent_term.astype(jnp.bfloat16), "ctx", scatter_dimension=1, tiled=True
        ).astype(jnp.float32),
        lax.psum_scatter(
            rope_term.astype(jnp.bfloat16), "ctx", scatter_dimension=2, tiled=True
        ).astype(jnp.float32),
    )
    latent_total, rope_total = (
        lax.psum(latent_part.astype(jnp.bfloat16), "ep").astype(jnp.float32),
        lax.psum(rope_part.astype(jnp.bfloat16), "ep").astype(jnp.float32),
    )
    latent_kgrad = latent_total.astype(jnp.bfloat16)
    rope_kgrad = rope_total.astype(jnp.bfloat16)
    return (attended, latent_qgrad, rope_qgrad, latent_kgrad, rope_kgrad)


def solution(mesh):
    placed = (
        P(None, "ctx", "ep", None),
        P(None, "ep", None, "ctx"),
        P(None, "ctx", None),
        P(None, None, "ctx"),
        P(None, "ctx", "ep", None),
    )
    return jax.shard_map(
        body,
        mesh=mesh,
        in_specs=placed,
        out_specs=(
            P(None, "ctx", "ep", None),
            P(None, "ctx", "ep", None),
            P(None, "ep", None, "ctx"),
            P(None, "ctx", None),
            P(None, None, "ctx"),
        ),
        check_vma=False,
    )
```

profile of v0, /device:TPU:0, one launch (start us, length us, event | category | flops | bytes accessed | tf_op | source)
XLA Modules:
  0.0 172.1 jit_solution(7928292447915737085)
XLA Ops:
  7.2 0.0 reduce-scatter.5.cloned.1.call-start
  7.2 9.0 %all_gather.6 = bf16[1,512,512]{2,1,0:T(8,128)(2,1)S(1)} all-gather(bf16[1,128,512]{2,1,0:T(8,128)(2,1)} %param.7), channel_id=1, replica_groups=mesh['ctx'=4,'ep'=8] {'ctx'}, dimensions={1}, use_global_device_ids=true | all-gather | bytes 655360 | tf_op jit(solution)/shard_map/all_gather | solution.py:12
  16.2 5.5 %all_gather.7 = bf16[1,64,512]{2,1,0:T(8,128)(2,1)S(1)} all-gather(bf16[1,64,128]{2,1,0:T(8,128)(2,1)} %param.8), channel_id=1, replica_groups=mesh['ctx'=4,'ep'=8] {'ctx'}, dimensions={2}, use_global_device_ids=true | all-gather | bytes 81920 | tf_op jit(solution)/shard_map/all_gather | solution.py:13
  21.7 0.1 iota_compare_fusion
  21.7 2.8 %fusion.23 = f32[512,128,16]{1,0,2:T(8,128)S(1)} fusion(bf16[128,16,512]{2,1,0:T(8,128)(2,1)S(1)} %bitcast.149, bf16[1,512,512]{2,1,0:T(8,128)(2,1)S(1)} %all_gather.6), kind=kOutput, calls=%fused_computation.26 | convolution fusion | flops 1073741824 | bytes 6815744 | tf_op jit(solution)/shard_map/sthd,sjd->shtj/dot_general | solution.py:19
  24.6 0.9 fusion.90
  25.5 0.6 fusion.5
  26.1 2.6 %fusion.91 = (f32[16,128,512]{2,1,0:T(8,128)S(1)}, bf16[16,128,512]{2,1,0:T(8,128)(2,1)}) fusion(bf16[1,512,512]{2,1,0:T(8,128)(2,1)S(1)} %all_gather.6, f32[16,128]{1,0:T(8,128)S(1)} %fusion.5, f32[1,16,128,512]{2,3,1,0:T(8,128)S(1)} %get-tuple-element.16, f32[16,128]{1,0:T(8,128)S(1)} %get-tuple-element.15), kind=kOutput, calls=%fused_computation.56 | convolution fusion | flops 1078984704 | bytes 11026432 | tf_op jit(solution)/shard_map/shtj,sjd->sthd/dot_general | solution.py:30
  28.7 0.2 copy-done.4
  28.9 2.4 %multiply_reduce_fusion = f32[16,128]{0,1:T(8,128)S(1)} fusion(f32[16,128,512]{2,1,0:T(8,128)S(1)} %get-tuple-element.17, bf16[1,128,16,512]{3,2,1,0:T(8,128)(2,1)S(1)} %copy-done.4), kind=kLoop, calls=%fused_computation.6 | loop fusion | flops 3143680 | bytes 6299648
  31.3 0.1 copy.40
  31.4 5.8 %fusion.28 = f32[512,512]{1,0:T(8,128)S(1)} fusion(bf16[128,16,512]{2,1,0:T(8,128)(2,1)} %bitcast.151, f32[16,128]{1,0:T(8,128)S(1)} %fusion.5, f32[1,16,128,512]{2,3,1,0:T(8,128)} %copy-done.2, f32[16,128]{1,0:T(8,128)S(1)} %get-tuple-element.15), kind=kOutput, calls=%fused_computation.29 | convolution fusion | flops 1076887552 | bytes 7356416 | tf_op jit(solution)/shard_map/shtj,sthd->sjd/dot_general | solution.py:51
  37.2 3.6 %fusion.1 = bf16[1,16,128,512]{2,3,1,0:T(8,128)(2,1)S(1)} fusion(f32[16,128]{1,0:T(8,128)S(1)} %copy.40, bf16[128,16,512]{2,1,0:T(8,128)(2,1)S(1)} %bitcast.152, f32[16,128]{1,0:T(8,128)S(1)} %fusion.5, f32[1,16,128,512]{2,3,1,0:T(8,128)S(1)} %copy-done.3, f32[16,128]{1,0:T(8,128)S(1)} %get-tuple-element.15, bf16[1,512,512]{2,1,0:T(8,128)(2,1)S(1)} %all_gather.6), kind=kOutput, calls=%fused_computation.2 | convolution fusion | flops 1078984704 | bytes 8937472 | tf_op jit(solution)/shard_map/sthd,sjd->shtj/dot_general | solution.py:36
  40.8 1.3 copy-done.1
  42.1 3.4 %fusion.53 = bf16[1,512,512]{2,1,0:T(8,128)(2,1)} fusion(f32[512,512]{1,0:T(8,128)S(1)} %fusion.28, bf16[128,16,512]{2,1,0:T(8,128)(2,1)S(1)} %bitcast.150, bf16[1,16,128,512]{2,3,1,0:T(8,128)(2,1)S(1)} %fusion.1), kind=kOutput, calls=%fused_computation.34 | convolution fusion | flops 1074528256 | bytes 5767168 | tf_op jit(solution)/shard_map/shtj,sthd->sjd/dot_general | solution.py:48
  45.5 0.0 reduce-scatter.5.cloned.1.call-update
  45.5 0.0 reduce-scatter.7.cloned.1.call-start
  45.6 2.3 %fusion.77 = bf16[1,64,512]{2,1,0:T(8,128)(2,1)S(1)} fusion(bf16[1,16,128,512]{2,3,1,0:T(8,128)(2,1)} %copy-done.1, bf16[1,16,64,128]{3,2,1,0:T(8,128)(2,1)S(1)} %copy-done.7), kind=kOutput, calls=%fused_computation.42 | convolution fusion | flops 134283264 | bytes 2424832 | tf_op jit(solution)/shard_map/shtj,shdt->sdj/dot_general | solution.py:54
  47.9 0.2 copy.44
  48.1 0.7 copy.69
  48.8 0.0 all-reduce.2.cloned.1.call-start
  48.9 4.2 %fusion.25 = bf16[1,128,16,512]{3,1,2,0:T(8,128)(2,1)} fusion(bf16[1,16,128,512]{2,3,1,0:T(8,128)(2,1)} %copy-done.1, bf16[1,512,512]{2,1,0:T(8,128)(2,1)S(1)} %all_gather.6), kind=kOutput, calls=%fused_computation.28 | convolution fusion | flops 1075838976 | bytes 4718592 | tf_op jit(solution)/shard_map/shtj,sjd->sthd/dot_general | solution.py:42
  53.1 15.1 %reduce-scatter.5.cloned.1.call-done = bf16[1,128,512]{2,1,0:T(8,128)(2,1)} async-done(((bf16[1,512,512]{2,1,0:T(8,128)(2,1)}), bf16[1,128,512]{2,1,0:T(8,128)(2,1)}) %reduce-scatter.5.cloned.1.call-update) | async-done | bytes 131088 | tf_op jit(solution)/shard_map/reduce_scatter | solution.py:58
  68.3 2.9 %fusion.65 = bf16[1,16,64,128]{3,2,1,0:T(8,128)(2,1)} fusion(bf16[1,16,128,512]{2,3,1,0:T(8,128)(2,1)} %copy-done.1, bf16[1,64,512]{2,1,0:T(8,128)(2,1)S(1)} %all_gather.7), kind=kOutput, calls=%fused_computation.38 | convolution fusion | flops 134479872 | bytes 2424832 | tf_op jit(solution)/shard_map/shtj,sdj->shdt/dot_general | solution.py:46
  71.2 4.1 %copy.31 = bf16[1,128,16,512]{3,2,1,0:T(8,128)(2,1)} copy(bf16[1,128,16,512]{3,1,2,0:T(8,128)(2,1)} %fusion.25) | data formatting | bytes 4194304
  75.3 2.5 %copy.30 = bf16[1,128,16,512]{3,2,1,0:T(8,128)(2,1)} copy(bf16[1,128,16,512]{3,1,2,0:T(8,128)(2,1)S(1)} %bitcast.153) | data formatting | bytes 4194304
  77.8 13.2 %reduce-scatter.7.cloned.1.call-done = bf16[128,64]{1,0:T(8,128)(2,1)} async-done(((bf16[512,64]{1,0:T(8,128)(2,1)}), bf16[128,64]{1,0:T(8,128)(2,1)}) %reduce-scatter.7.cloned.1.call-update) | async-done | bytes 16400
  91.0 0.8 reshape_bitcast_fusion
  91.8 0.1 copy.45
  91.9 37.7 %psum.15 = bf16[1,64,128]{2,1,0:T(8,128)(2,1)} all-reduce(bf16[1,64,128]{2,1,0:T(8,128)(2,1)S(1)} %copy.45), channel_id=1, replica_groups=mesh['ctx'=4,'ep'=8] {'ep'}, use_global_device_ids=true, to_apply=%region_5.6 | all-reduce | flops 8192 | bytes 32768 | tf_op jit(solution)/shard_map/psum | solution.py:67
  129.6 34.5 %all-reduce.2.cloned.1.call-done = bf16[1,128,512]{2,1,0:T(8,128)(2,1)} async-done(((bf16[1,128,512]{2,1,0:T(8,128)(2,1)}), bf16[1,128,512]{2,1,0:T(8,128)(2,1)}) %all-reduce.2.cloned.1.call-update) | async-done | bytes 131088 | tf_op jit(solution)/shard_map/psum | solution.py:66
  164.0 1.6 copy.71
  (17 shorter events, 0.1 us)
Async XLA Ops:
  7.2 14.6 %copy-start = (bf16[1,128,16,512]{3,2,1,0:T(8,128)(2,1)S(1)}, bf16[1,128,16,512]{3,2,1,0:T(8,128)(2,1)}, u32[]{:S(2)}) copy-start(bf16[1,128,16,512]{3,2,1,0:T(8,128)(2,1)} %param.5) | copy-start | bytes 6291460
  7.2 61.1 %reduce-scatter.5.cloned.1.call-start = ((), (), s32[]{:S(2)}) async-start(), calls=%async_computation.2 | async-start | bytes 655360 | tf_op jit(solution)/shard_map/reduce_scatter | solution.py:58
  21.7 2.8 %copy-start.7 = (bf16[1,16,64,128]{3,2,1,0:T(8,128)(2,1)S(1)}, bf16[1,16,64,128]{3,2,1,0:T(8,128)(2,1)}, u32[]{:S(2)}) copy-start(bf16[1,16,64,128]{3,2,1,0:T(8,128)(2,1)} %param.6) | copy-start | bytes 786436
  25.5 3.3 %copy-start.2 = (f32[1,16,128,512]{2,3,1,0:T(8,128)}, f32[1,16,128,512]{2,3,1,0:T(8,128)S(1)}, u32[]{:S(2)}) copy-start(f32[1,16,128,512]{2,3,1,0:T(8,128)S(1)} %get-tuple-element.16) | copy-start | bytes 12582916
  26.1 2.9 %copy-start.4 = (bf16[1,128,16,512]{3,2,1,0:T(8,128)(2,1)S(1)}, bf16[1,128,16,512]{3,2,1,0:T(8,128)(2,1)}, u32[]{:S(2)}) copy-start(bf16[1,128,16,512]{3,2,1,0:T(8,128)(2,1)} %param.9) | copy-start | bytes 6291460
  31.4 5.8 %copy-start.3 = (f32[1,16,128,512]{2,3,1,0:T(8,128)S(1)}, f32[1,16,128,512]{2,3,1,0:T(8,128)}, u32[]{:S(2)}) copy-start(f32[1,16,128,512]{2,3,1,0:T(8,128)} %copy-done.2) | copy-start | bytes 12582916
  31.4 5.8 %copy-start.5 = (bf16[1,128,16,512]{3,2,1,0:T(8,128)(2,1)S(1)}, bf16[1,128,16,512]{3,2,1,0:T(8,128)(2,1)}, u32[]{:S(2)}) copy-start(bf16[1,128,16,512]{3,2,1,0:T(8,128)(2,1)} %param.9) | copy-start | bytes 6291460
  40.8 1.3 copy-start.1
  45.5 45.5 %reduce-scatter.7.cloned.1.call-start = ((), (), s32[]{:S(2)}) async-start(), calls=%async_computation.4 | async-start | bytes 163840
  48.8 115.2 %all-reduce.2.cloned.1.call-start = ((), (), s32[]{:S(2)}) async-start(), calls=%async_computation.3 | async-start | bytes 262144 | tf_op jit(solution)/shard_map/psum | solution.py:66
  68.3 7.0 %copy-start.6 = (bf16[16,128,512]{2,1,0:T(8,128)(2,1)S(1)}, bf16[16,128,512]{2,1,0:T(8,128)(2,1)}, u32[]{:S(2)}) copy-start(bf16[16,128,512]{2,1,0:T(8,128)(2,1)} %get-tuple-element.18) | copy-start | bytes 6291460
Sparse Core Ops, SparseCore 0:
  45.7 22.5 reduce-scatter.4
  71.4 19.5 reduce-scatter.6
  94.3 69.6 all-reduce.1
where the time goes:
time: 173 us; the launch traced here: 172 us
  waiting for transfers between devices  62.9 us (36%)
  blocking collectives  52.1 us (30%)
  matrix products  28.6 us (17%)
  between operations  13.9 us (8%)
  local copies, waits for them, and re-layouts  11.5 us (7%)
  other arithmetic  3.03 us (2%)
    psum x1, blocking collectives, body(): lax.psum(rope_part.astype(jnp.bfloat16), 'ep').astype(jnp.float32)  37.7 us
    psum x1, waiting for transfers between devices, body(): lax.psum(latent_part.astype(jnp.bfloat16), 'ep').astype(jnp.float32)  34.5 us
    reduce_scatter x1, waiting for transfers between devices, body(): lax.psum_scatter(latent_term.astype(jnp.bfloat16), 'ctx', scatter_dimensi...  15.1 us
    unnamed x4, waiting for transfers between devices  13.3 us
    unnamed x23, local copies, waits for them, and re-layouts  11.4 us
    all_gather x1, blocking collectives, body(): lax.all_gather(key_latent, 'ctx', axis=1, tiled=True)  8.96 us
    dot_general x1, matrix products, body(): jnp.einsum('shtj,sthd->sjd', rounded_weights, output_grad, preferred_elem...  5.81 us
    all_gather x1, blocking collectives, body(): lax.all_gather(key_rope, 'ctx', axis=2, tiled=True)  5.46 us
  transfers between devices with their start and end apart: 3, of which 3 were waited for; matrix products, arithmetic and copies ran while one was open for 10% of the time, Pallas kernels for 0%

commit v1 on v0

--- a/solution.py
+++ b/solution.py
@@ -4,6 +4,11 @@
 from jax.sharding import PartitionSpec as P
 
 scale_factor = 192.0 ** (-0.5)
+
+
+def resolve_members_all_over_axis(my_data):
+    block_now = jax.lax.all_gather(my_data, "ep")
+    return jnp.sum(block_now, axis=0)
 
 
 def body(query_latent, query_rope, key_latent, key_rope, output_grad):
@@ -63,7 +68,7 @@
         ).astype(jnp.float32),
     )
     latent_total, rope_total = (
-        lax.psum(latent_part.astype(jnp.bfloat16), "ep").astype(jnp.float32),
+        resolve_members_all_over_axis(latent_part.astype(jnp.bfloat16)).astype(jnp.float32),
         lax.psum(rope_part.astype(jnp.bfloat16), "ep").astype(jnp.float32),
     )
     latent_kgrad = latent_total.astype(jnp.bfloat16)

time: 173 us -> 142 us (0.82)
  waiting for transfers between devices: 62.9 us -> 36.4 us
  local copies, waits for them, and re-layouts: 11.5 us -> 8.34 us
  matrix products: 28.6 us -> 25.7 us
  other arithmetic: 3.03 us -> 5.09 us
    psum x1 -> x0, waiting for transfers between devices: 34.5 us -> none  [body(): lax.psum(latent_part.astype(jnp.bfloat16), 'ep').astype(jnp.float32)]
    reduce_scatter x1, waiting for transfers between devices: 15.1 us -> 19.4 us  [body(): lax.psum_scatter(latent_term.astype(jnp.bfloat16), 'ctx', scatter_dimensi...]
    all_gather x0 -> x1, waiting for transfers between devices: none -> 3.44 us  [resolve_members_all_over_axis(): block_now = jax.lax.all_gather(my_data, 'ep')]
    unnamed x23 -> x24, local copies, waits for them, and re-layouts: 11.4 us -> 8.27 us
    reduce_sum x0 -> x1, other arithmetic: none -> 2.06 us  [resolve_members_all_over_axis(): return jnp.sum(block_now, axis=0)]
    dot_general x1, matrix products: 2.93 us -> 1.19 us  [body(): jnp.einsum('shtj,sdj->shdt', score_grad, whole_rope, preferred_element_ty...]
  transfers between devices with their start and end apart: 3 -> 3, of which waited for: 3 -> 3; matrix products, arithmetic and copies ran while one was open for 10% -> 9% of each run, Pallas kernels for 0% -> 0%
where the time goes in v1:
time: 142 us
  blocking collectives  52.5 us (37%)
  waiting for transfers between devices  36.4 us (26%)
  matrix products  25.7 us (18%)
  between operations  13.9 us (10%)
  local copies, waits for them, and re-layouts  8.34 us (6%)
  other arithmetic  5.09 us (4%)
    psum x1, blocking collectives, body(): lax.psum(rope_part.astype(jnp.bfloat16), 'ep').astype(jnp.float32)  38.1 us
    reduce_scatter x1, waiting for transfers between devices, body(): lax.psum_scatter(latent_term.astype(jnp.bfloat16), 'ctx', scatter_dimensi...  19.4 us
    unnamed x4, waiting for transfers between devices  13.6 us
    all_gather x1, blocking collectives, body(): lax.all_gather(key_latent, 'ctx', axis=1, tiled=True)  8.96 us
    unnamed x24, local copies, waits for them, and re-layouts  8.27 us
    dot_general x1, matrix products, body(): jnp.einsum('shtj,sthd->sjd', rounded_weights, output_grad, preferred_elem...  5.81 us
    all_gather x1, blocking collectives, body(): lax.all_gather(key_rope, 'ctx', axis=2, tiled=True)  5.46 us
    dot_general x1, matrix products, body(): jnp.einsum('sthd,sjd->shtj', output_grad, whole_latent, preferred_element...  3.58 us
  transfers between devices with their start and end apart: 3, of which 3 were waited for; matrix products, arithmetic and copies ran while one was open for 9% of the time, Pallas kernels for 0%

profile of v1, /device:TPU:0, one launch (start us, length us, event | category | flops | bytes accessed | tf_op | source)
XLA Modules:
  0.0 142.0 jit_solution(3787447948937611190)
XLA Ops:
  7.2 0.0 reduce-scatter.5.cloned.1.call-start
  7.2 9.0 %all_gather.12 = bf16[1,512,512]{2,1,0:T(8,128)(2,1)S(1)} all-gather(bf16[1,128,512]{2,1,0:T(8,128)(2,1)} %param.7), channel_id=1, replica_groups=mesh['ctx'=4,'ep'=8] {'ctx'}, dimensions={1}, use_global_device_ids=true | all-gather | bytes 655360 | tf_op jit(solution)/shard_map/all_gather | solution.py:17
  16.2 5.5 %all_gather.13 = bf16[1,64,512]{2,1,0:T(8,128)(2,1)S(1)} all-gather(bf16[1,64,128]{2,1,0:T(8,128)(2,1)} %param.8), channel_id=1, replica_groups=mesh['ctx'=4,'ep'=8] {'ctx'}, dimensions={2}, use_global_device_ids=true | all-gather | bytes 81920 | tf_op jit(solution)/shard_map/all_gather | solution.py:18
  21.7 0.1 iota_compare_fusion
  21.7 2.8 %fusion.23 = f32[512,128,16]{1,0,2:T(8,128)S(1)} fusion(bf16[128,16,512]{2,1,0:T(8,128)(2,1)S(1)} %bitcast.150, bf16[1,512,512]{2,1,0:T(8,128)(2,1)S(1)} %all_gather.12), kind=kOutput, calls=%fused_computation.26 | convolution fusion | flops 1073741824 | bytes 6815744 | tf_op jit(solution)/shard_map/sthd,sjd->shtj/dot_general | solution.py:24
  24.6 0.9 fusion.90
  25.5 0.6 fusion.5
  26.1 2.6 %fusion.91 = (f32[16,128,512]{2,1,0:T(8,128)S(1)}, bf16[16,128,512]{2,1,0:T(8,128)(2,1)}) fusion(bf16[1,512,512]{2,1,0:T(8,128)(2,1)S(1)} %all_gather.12, f32[16,128]{1,0:T(8,128)S(1)} %fusion.5, f32[1,16,128,512]{2,3,1,0:T(8,128)S(1)} %get-tuple-element.16, f32[16,128]{1,0:T(8,128)S(1)} %get-tuple-element.15), kind=kOutput, calls=%fused_computation.56 | convolution fusion | flops 1078984704 | bytes 11026432 | tf_op jit(solution)/shard_map/shtj,sjd->sthd/dot_general | solution.py:35
  28.7 0.2 copy-done.5
  28.9 2.4 %multiply_reduce_fusion = f32[16,128]{0,1:T(8,128)S(1)} fusion(f32[16,128,512]{2,1,0:T(8,128)S(1)} %get-tuple-element.17, bf16[1,128,16,512]{3,2,1,0:T(8,128)(2,1)S(1)} %copy-done.5), kind=kLoop, calls=%fused_computation.6 | loop fusion | flops 3143680 | bytes 6299648
  31.3 0.1 copy.40
  31.4 5.8 %fusion.28 = f32[512,512]{1,0:T(8,128)S(1)} fusion(bf16[128,16,512]{2,1,0:T(8,128)(2,1)} %bitcast.152, f32[16,128]{1,0:T(8,128)S(1)} %fusion.5, f32[1,16,128,512]{2,3,1,0:T(8,128)} %copy-done.3, f32[16,128]{1,0:T(8,128)S(1)} %get-tuple-element.15), kind=kOutput, calls=%fused_computation.29 | convolution fusion | flops 1076887552 | bytes 7356416 | tf_op jit(solution)/shard_map/shtj,sthd->sjd/dot_general | solution.py:56
  37.2 3.6 %fusion.1 = bf16[1,16,128,512]{2,3,1,0:T(8,128)(2,1)S(1)} fusion(f32[16,128]{1,0:T(8,128)S(1)} %copy.40, bf16[128,16,512]{2,1,0:T(8,128)(2,1)S(1)} %bitcast.153, f32[16,128]{1,0:T(8,128)S(1)} %fusion.5, f32[1,16,128,512]{2,3,1,0:T(8,128)S(1)} %copy-done.4, f32[16,128]{1,0:T(8,128)S(1)} %get-tuple-element.15, bf16[1,512,512]{2,1,0:T(8,128)(2,1)S(1)} %all_gather.12), kind=kOutput, calls=%fused_computation.2 | convolution fusion | flops 1078984704 | bytes 8937472 | tf_op jit(solution)/shard_map/sthd,sjd->shtj/dot_general | solution.py:41
  40.8 1.3 copy-done.1
  42.2 3.4 %fusion.53 = bf16[1,512,512]{2,1,0:T(8,128)(2,1)} fusion(f32[512,512]{1,0:T(8,128)S(1)} %fusion.28, bf16[128,16,512]{2,1,0:T(8,128)(2,1)S(1)} %bitcast.151, bf16[1,16,128,512]{2,3,1,0:T(8,128)(2,1)S(1)} %fusion.1), kind=kOutput, calls=%fused_computation.34 | convolution fusion | flops 1074528256 | bytes 5767168 | tf_op jit(solution)/shard_map/shtj,sthd->sjd/dot_general | solution.py:53
  45.6 0.0 reduce-scatter.7.cloned.1.call-start
  45.6 2.3 %fusion.77 = bf16[1,64,512]{2,1,0:T(8,128)(2,1)S(1)} fusion(bf16[1,16,128,512]{2,3,1,0:T(8,128)(2,1)} %copy-done.1, bf16[1,16,64,128]{3,2,1,0:T(8,128)(2,1)S(1)} %copy-done.8), kind=kOutput, calls=%fused_computation.42 | convolution fusion | flops 134283264 | bytes 2424832 | tf_op jit(solution)/shard_map/shtj,shdt->sdj/dot_general | solution.py:59
  48.0 0.2 copy.44
  48.1 0.7 copy.69
  48.8 0.0 all-gather.3.cloned.1.call-start
  48.9 19.4 %reduce-scatter.5.cloned.1.call-done = bf16[1,128,512]{2,1,0:T(8,128)(2,1)} async-done(((bf16[1,512,512]{2,1,0:T(8,128)(2,1)}), bf16[1,128,512]{2,1,0:T(8,128)(2,1)}) %reduce-scatter.5.cloned.1.call-update) | async-done | bytes 131088 | tf_op jit(solution)/shard_map/reduce_scatter | solution.py:63
  68.2 0.0 all-gather.3.cloned.1.call-update
  68.3 3.0 %fusion.25 = bf16[1,128,16,512]{3,1,2,0:T(8,128)(2,1)S(1)} fusion(bf16[1,16,128,512]{2,3,1,0:T(8,128)(2,1)} %copy-done.1, bf16[1,512,512]{2,1,0:T(8,128)(2,1)S(1)} %all_gather.12), kind=kOutput, calls=%fused_computation.28 | convolution fusion | flops 1075838976 | bytes 4718592 | tf_op jit(solution)/shard_map/shtj,sjd->sthd/dot_general | solution.py:47
  71.3 2.5 %copy.31 = bf16[1,128,16,512]{3,2,1,0:T(8,128)(2,1)} copy(bf16[1,128,16,512]{3,1,2,0:T(8,128)(2,1)S(1)} %fusion.25) | data formatting | bytes 4194304
  73.8 2.5 %copy.30 = bf16[1,128,16,512]{3,2,1,0:T(8,128)(2,1)} copy(bf16[1,128,16,512]{3,1,2,0:T(8,128)(2,1)S(1)} %bitcast.154) | data formatting | bytes 4194304
  76.3 1.2 fusion.65
  77.5 13.5 %reduce-scatter.7.cloned.1.call-done = bf16[128,64]{1,0:T(8,128)(2,1)} async-done(((bf16[512,64]{1,0:T(8,128)(2,1)}), bf16[128,64]{1,0:T(8,128)(2,1)}) %reduce-scatter.7.cloned.1.call-update) | async-done | bytes 16400
  91.0 0.8 reshape_bitcast_fusion
  91.8 0.1 copy.45
  91.9 38.1 %psum.7 = bf16[1,64,128]{2,1,0:T(8,128)(2,1)} all-reduce(bf16[1,64,128]{2,1,0:T(8,128)(2,1)S(1)} %copy.45), channel_id=1, replica_groups=mesh['ctx'=4,'ep'=8] {'ep'}, use_global_device_ids=true, to_apply=%region_5.6 | all-reduce | flops 8192 | bytes 32768 | tf_op jit(solution)/shard_map/psum | solution.py:72
  129.9 3.4 %all-gather.3.cloned.1.call-done = bf16[8,128,512]{2,1,0:T(8,128)(2,1)} async-done(((bf16[1,128,512]{2,1,0:T(8,128)(2,1)}), bf16[8,128,512]{2,1,0:T(8,128)(2,1)}) %all-gather.3.cloned.1.call-update) | async-done | bytes 1048592 | tf_op jit(solution)/shard_map/all_gather | solution.py:10
  133.4 2.1 %reduce.4 = bf16[128,512]{1,0:T(8,128)(2,1)} reduce(bf16[8,128,512]{2,1,0:T(8,128)(2,1)} %all-gather.3.cloned.1.call-done, bf16[]{:T(256)} %constant.5.clone.1), dimensions={0}, to_apply=%region_3.4 | reduce | flops 458752 | bytes 1179650 | tf_op jit(solution)/shard_map/reduce_sum | solution.py:11
  (19 shorter events, 0.1 us)
Async XLA Ops:
  7.2 14.6 %copy-start = (bf16[1,128,16,512]{3,2,1,0:T(8,128)(2,1)S(1)}, bf16[1,128,16,512]{3,2,1,0:T(8,128)(2,1)}, u32[]{:S(2)}) copy-start(bf16[1,128,16,512]{3,2,1,0:T(8,128)(2,1)} %param.5) | copy-start | bytes 6291460
  7.2 61.1 %reduce-scatter.5.cloned.1.call-start = ((), (), s32[]{:S(2)}) async-start(), calls=%async_computation.2 | async-start | bytes 655360 | tf_op jit(solution)/shard_map/reduce_scatter | solution.py:63
  21.7 2.8 %copy-start.8 = (bf16[1,16,64,128]{3,2,1,0:T(8,128)(2,1)S(1)}, bf16[1,16,64,128]{3,2,1,0:T(8,128)(2,1)}, u32[]{:S(2)}) copy-start(bf16[1,16,64,128]{3,2,1,0:T(8,128)(2,1)} %param.6) | copy-start | bytes 786436
  25.5 3.3 %copy-start.3 = (f32[1,16,128,512]{2,3,1,0:T(8,128)}, f32[1,16,128,512]{2,3,1,0:T(8,128)S(1)}, u32[]{:S(2)}) copy-start(f32[1,16,128,512]{2,3,1,0:T(8,128)S(1)} %get-tuple-element.16) | copy-start | bytes 12582916
  26.1 2.9 %copy-start.5 = (bf16[1,128,16,512]{3,2,1,0:T(8,128)(2,1)S(1)}, bf16[1,128,16,512]{3,2,1,0:T(8,128)(2,1)}, u32[]{:S(2)}) copy-start(bf16[1,128,16,512]{3,2,1,0:T(8,128)(2,1)} %param.9) | copy-start | bytes 6291460
  31.4 5.8 %copy-start.4 = (f32[1,16,128,512]{2,3,1,0:T(8,128)S(1)}, f32[1,16,128,512]{2,3,1,0:T(8,128)}, u32[]{:S(2)}) copy-start(f32[1,16,128,512]{2,3,1,0:T(8,128)} %copy-done.3) | copy-start | bytes 12582916
  31.4 5.8 %copy-start.6 = (bf16[1,128,16,512]{3,2,1,0:T(8,128)(2,1)S(1)}, bf16[1,128,16,512]{3,2,1,0:T(8,128)(2,1)}, u32[]{:S(2)}) copy-start(bf16[1,128,16,512]{3,2,1,0:T(8,128)(2,1)} %param.9) | copy-start | bytes 6291460
  40.8 1.4 copy-start.1
  45.6 45.4 %reduce-scatter.7.cloned.1.call-start = ((), (), s32[]{:S(2)}) async-start(), calls=%async_computation.4 | async-start | bytes 163840
  48.8 84.6 %all-gather.3.cloned.1.call-start = ((), (), s32[]{:S(2)}) async-start(), calls=%async_computation.3 | async-start | bytes 1179648 | tf_op jit(solution)/shard_map/all_gather | solution.py:10
  68.3 5.5 %copy-start.7 = (bf16[16,128,512]{2,1,0:T(8,128)(2,1)S(1)}, bf16[16,128,512]{2,1,0:T(8,128)(2,1)}, u32[]{:S(2)}) copy-start(bf16[16,128,512]{2,1,0:T(8,128)(2,1)} %get-tuple-element.18) | copy-start | bytes 6291460
  71.3 5.0 %copy-start.2 = (bf16[1,16,128,512]{2,3,1,0:T(8,128)(2,1)S(1)}, bf16[1,16,128,512]{2,3,1,0:T(8,128)(2,1)}, u32[]{:S(2)}) copy-start(bf16[1,16,128,512]{2,3,1,0:T(8,128)(2,1)} %copy-done.1) | copy-start | bytes 6291460
Sparse Core Ops, SparseCore 0:
  45.7 22.5 reduce-scatter.4
  71.4 19.5 reduce-scatter.6
  93.1 40.2 all-gather.2
